TPU v7x, 256 devices: a whole 4x4x8 slice. The times are simulated.
256 devices in a mesh: docs: 32 (over y, x, z_hi), dims: 8 (over z_lo, core).
Axes of the slice: x: 4, y: 4, z: 8 (z_hi: 2, z_lo: 4; z = z_hi * 4 + z_lo), core: 2. Of those that a mesh axis runs over, the one named last changes fastest.
Arguments:
- queries: bfloat16 [16384, 3072], P('docs', 'dims'), may hold values from -6 to 6
- doc_vectors: bfloat16 [65536, 3072], P('docs', 'dims'), may hold values from -6 to 6
- surv_pairs: int32 [32, 144], P('docs'), may hold values from 0 to 2047
- surv_count: int32 [32], P('docs'), may hold values from 36 to 144, as said below
- short_pairs: int32 [32, 96], P('docs'), may hold values from 0 to 2047
- short_count: int32 [32], P('docs'), may hold values from 24 to 96, as said below
Outputs:
- prefix_scores: float32 [32, 144, 128, 128], P('docs', None, 'dims')
- full_scores: float32 [32, 96, 128, 128], P('docs', None, 'dims')
Inputs may be any that keep to these rules, and one draw needn't show every extreme that they name: `surv_count`: each shard's live survivor slots; some shard has all 144 slots live. `short_count`: each shard's live shortlist slots; some shard has all 96 slots live.
All inputs are finite; a program needn't handle non-finite values.
Results may differ from a plain program's by a relative error of at most 0.0003.
Values may be sent and summed in bfloat16 or wider, within the bound.
No kernel may reach another device: no remote copies, remote signals or barrier semaphores. Data moves between devices by JAX's collectives and lax.ppermute only.
A program may use at most 128 MiB of HBM per device.

v0:
```python
import jax
import jax.numpy as jnp
from jax import lax
from jax.sharding import Mesh
from jax.sharding import PartitionSpec as P

D = 3072
PREFIX = 768
QB = 128
DB = 128
DOCS_PARTS = (("y", 4), ("x", 4), ("zh", 2))
DIMS_PARTS = (("zl", 4), ("c", 2))
DOCS = tuple((name for name, _ in DOCS_PARTS))
DIMS = tuple((name for name, _ in DIMS_PARTS))


def shards(queries, doc_vectors, surv_pairs, surv_count, short_pairs, short_count):
    near = lax.all_gather(queries, "zh", axis=0, tiled=True)
    every_query = lax.all_gather(near, ("y", "x"), axis=0, tiled=True)
    slice_width = queries.shape[1]
    query_blocks = every_query.reshape(-1, QB, slice_width)
    doc_blocks = doc_vectors.reshape(-1, DB, slice_width)
    local_blocks = doc_blocks.shape[0]
    columns = lax.axis_index(DIMS) * slice_width + jnp.arange(slice_width)
    prefix_blocks = jnp.where(
        columns[None, None, :] < PREFIX, doc_blocks, jnp.zeros((), doc_blocks.dtype)
    )

    def pair_products(pair_ids, doc_side):
        picked_queries = jnp.take(query_blocks, pair_ids // local_blocks, axis=0)
        picked_docs = jnp.take(doc_side, pair_ids % local_blocks, axis=0)
        return jnp.einsum(
            "gqc,gdc->gqd", picked_queries, picked_docs, preferred_element_type=jnp.float32
        )

    full_terms = pair_products(short_pairs[0], doc_blocks)
    prefix_terms = pair_products(surv_pairs[0], prefix_blocks)
    prefix_sum, full_sum = (
        lax.psum_scatter(prefix_terms, DIMS, scatter_dimension=1, tiled=True),
        lax.psum_scatter(full_terms, DIMS, scatter_dimension=1, tiled=True),
    )

    def finish(summed, live_count, factor):
        slots = jnp.arange(summed.shape[0])
        return jnp.where(slots[:, None, None] < live_count, summed * factor, jnp.float32(0.0))

    prefix_out = finish(prefix_sum, surv_count[0], float(PREFIX) ** (-0.5))
    full_out = finish(full_sum, short_count[0], float(D) ** (-0.5))
    return (prefix_out[None], full_out[None])


def solution(mesh):
    sizes = [n for _, n in DOCS_PARTS + DIMS_PARTS]
    assert mesh.devices.size == jnp.prod(jnp.array(sizes))
    parts = Mesh(mesh.devices.reshape(sizes), DOCS + DIMS)
    placed = (P(DOCS, DIMS), P(DOCS, DIMS), P(DOCS, None), P(DOCS), P(DOCS, None), P(DOCS))
    return jax.shard_map(
        shards,
        mesh=parts,
        in_specs=placed,
        out_specs=(P(DOCS, None, DIMS, None), P(DOCS, None, DIMS, None)),
        check_vma=False,
    )
```

profile of v0, /device:TPU:2, one launch (start us, length us, event | category | flops | bytes accessed | tf_op | source)
XLA Modules:
  0.0 341.6 jit_solution(15398356191512357973)
XLA Ops:
  7.2 0.0 all-gather.2.cloned.1.call-start
  7.2 23.2 %all_gather.6 = bf16[1024,384]{1,0:T(8,128)(2,1)} all-gather(bf16[512,384]{1,0:T(8,128)(2,1)} %param.6), channel_id=1, replica_groups=mesh['y'=4,'x'=4,'zh'=2,'zl'=4,'c'=2] {'zh'}, dimensions={0}, use_global_device_ids=true | all-gather | bytes 1179648 | tf_op jit(solution)/shard_map/all_gather | solution.py:18
  30.4 0.0 all-gather.2.cloned.1.call-update
  30.5 0.0 reduce-scatter.5.cloned.1.call-start
  30.5 0.7 fusion.12
  31.2 0.0 copy-start.2
  31.2 9.3 %gather_fusion.3 = bf16[96,128,384]{2,1,0:T(8,128)(2,1)} fusion(bf16[16,128,384]{2,1,0:T(8,128)(2,1)} %bitcast.65, s32[1024]{0:T(1024)S(1)} %get-tuple-element.10), kind=kCustom, calls=%fused_computation.3 | custom fusion | bytes 18874752 | tf_op jit(solution)/shard_map/jit(_take)/gather | solution.py:31
  40.5 0.0 copy-done.2
  40.5 88.3 %all-gather.2.cloned.1.call-done = bf16[16384,384]{1,0:T(8,128)(2,1)} async-done(((bf16[1024,384]{1,0:T(8,128)(2,1)}), bf16[16384,384]{1,0:T(8,128)(2,1)}) %all-gather.2.cloned.1.call-update) | async-done | bytes 12582928 | tf_op jit(solution)/shard_map/all_gather | solution.py:19
  128.9 12.5 %gather_fusion.2 = bf16[96,128,384]{2,1,0:T(8,128)(2,1)} fusion(bf16[128,128,384]{2,1,0:T(8,128)(2,1)} %bitcast.67, s32[1024]{0:T(1024)S(1)} %get-tuple-element.11), kind=kCustom, calls=%fused_computation.2 | custom fusion | bytes 18874752 | tf_op jit(solution)/shard_map/jit(_take)/gather | solution.py:30
  141.4 10.4 %fusion.5 = f32[96,128,128]{2,1,0:T(8,128)} fusion(bf16[96,128,384]{2,1,0:T(8,128)(2,1)} %gather_fusion.3, bf16[96,128,384]{2,1,0:T(8,128)(2,1)} %gather_fusion.2, pred[96]{0:T(512)(128)(4,1)S(1)} %get-tuple-element.7, pred[96]{0:T(512)(128)(4,1)S(1)} %get-tuple-element.6), kind=kOutput, calls=%fused_computation.9 | convolution fusion | flops 1217396736 | bytes 25166016 | tf_op jit(solution)/shard_map/gqc,gdc->gqd/dot_general | solution.py:32
  151.8 0.0 reduce-scatter.5.cloned.1.call-update
  151.8 0.2 reduce-scatter.3.cloned.1.call-start
  152.1 0.0 copy-done.1
  152.1 0.0 copy-done
  152.1 0.2 broadcast_select_fusion
  152.3 9.5 %gather_fusion.1 = bf16[144,128,384]{2,1,0:T(8,128)(2,1)} fusion(bf16[16,128,384]{2,1,0:T(8,128)(2,1)S(1)} %broadcast_select_fusion, s32[1024]{0:T(1024)S(1)} %pad_clamp_fusion.2), kind=kCustom, calls=%fused_computation.1 | custom fusion | bytes 28312128 | tf_op jit(solution)/shard_map/jit(_take)/gather | solution.py:31
  161.8 14.7 %gather_fusion = bf16[144,128,384]{2,1,0:T(8,128)(2,1)} fusion(bf16[128,128,384]{2,1,0:T(8,128)(2,1)} %bitcast.68, s32[1024]{0:T(1024)S(1)} %pad_clamp_fusion.3), kind=kCustom, calls=%fused_computation | custom fusion | bytes 28312128 | tf_op jit(solution)/shard_map/jit(_take)/gather | solution.py:30
  176.5 14.9 %fusion = f32[144,128,128]{2,1,0:T(8,128)} fusion(bf16[144,128,384]{2,1,0:T(8,128)(2,1)} %gather_fusion.1, bf16[144,128,384]{2,1,0:T(8,128)(2,1)} %gather_fusion, pred[144]{0:T(512)(128)(4,1)S(1)} %get-tuple-element.5, pred[144]{0:T(512)(128)(4,1)S(1)} %get-tuple-element.4), kind=kOutput, calls=%fused_computation.4 | convolution fusion | flops 1826095104 | bytes 37749024 | tf_op jit(solution)/shard_map/gqc,gdc->gqd/dot_general | solution.py:32
  191.4 0.0 reduce-scatter.3.cloned.1.call-update
  192.7 34.0 %reduce-scatter.5.cloned.1.call-done = f32[96,16,128]{2,1,0:T(8,128)} async-done(((f32[96,128,128]{2,1,0:T(8,128)}), f32[96,16,128]{2,1,0:T(8,128)}) %reduce-scatter.5.cloned.1.call-update) | async-done | bytes 786448 | tf_op jit(solution)/shard_map/reduce_scatter | solution.py:40
  226.7 2.2 select_bitcast_fusion.1
  228.9 103.7 %reduce-scatter.3.cloned.1.call-done = f32[144,16,128]{2,1,0:T(8,128)} async-done(((f32[144,128,128]{2,1,0:T(8,128)}), f32[144,16,128]{2,1,0:T(8,128)}) %reduce-scatter.3.cloned.1.call-update) | async-done | bytes 1179664 | tf_op jit(solution)/shard_map/reduce_scatter | solution.py:39
  332.6 2.5 select_bitcast_fusion
  (12 shorter events, 0.1 us)
Async XLA Ops:
  7.2 121.7 %all-gather.2.cloned.1.call-start = ((), (), s32[]{:S(2)}) async-start(), calls=%async_computation.2 | async-start | bytes 13369344 | tf_op jit(solution)/shard_map/all_gather | solution.py:19
  30.5 196.3 %reduce-scatter.5.cloned.1.call-start = ((), (), s32[]{:S(2)}) async-start(), calls=%async_computation.4 | async-start | bytes 7077888 | tf_op jit(solution)/shard_map/reduce_scatter | solution.py:40
  31.2 9.3 %copy-start.2 = (s32[1,96]{1,0:T(1,128)S(1)}, s32[1,96]{1,0:T(1,128)}, u32[]{:S(2)}) copy-start(s32[1,96]{1,0:T(1,128)} %param.10) | copy-start | bytes 1156
  141.3 10.7 %copy-start.1 = (s32[1,144]{1,0:T(1,128)S(1)}, s32[1,144]{1,0:T(1,128)}, u32[]{:S(2)}) copy-start(s32[1,144]{1,0:T(1,128)} %param.8) | copy-start | bytes 1732
  141.3 10.8 %copy-start = (bf16[2048,384]{1,0:T(8,128)(2,1)S(1)}, bf16[2048,384]{1,0:T(8,128)(2,1)}, u32[]{:S(2)}) copy-start(bf16[2048,384]{1,0:T(8,128)(2,1)} %param.7) | copy-start | bytes 4718596
  151.8 180.8 %reduce-scatter.3.cloned.1.call-start = ((), (), s32[]{:S(2)}) async-start(), calls=%async_computation.3 | async-start | bytes 10616832 | tf_op jit(solution)/shard_map/reduce_scatter | solution.py:39
Sparse Core Ops, SparseCore 0:
  30.6 98.2 all-gather.1
  151.9 74.7 reduce-scatter.4
  229.3 103.2 reduce-scatter.2
where the time goes:
time: 342 us
  waiting for transfers between devices  226 us (66%)
  local copies, waits for them, and re-layouts  46 us (13%)
  matrix products  25.3 us (7%)
  blocking collectives  23.2 us (7%)
  between operations  15.1 us (4%)
  other arithmetic  5.6 us (2%)
    reduce_scatter x1, waiting for transfers between devices, shards(): lax.psum_scatter(prefix_terms, DIMS, scatter_dimension=1, tiled=True)  104 us
    all_gather x1, waiting for transfers between devices, shards(): every_query = lax.all_gather(near, ('y', 'x'), axis=0, tiled=True)  88.3 us
    reduce_scatter x1, waiting for transfers between devices, shards(): lax.psum_scatter(full_terms, DIMS, scatter_dimension=1, tiled=True)  34 us
    gather x2, local copies, waits for them, and re-layouts, pair_products(): picked_queries = jnp.take(query_blocks, pair_ids // local_blocks, axis=0)  27.2 us
    dot_general x2, matrix products, pair_products(): jnp.einsum('gqc,gdc->gqd', picked_queries, picked_docs, preferred_element...  25.3 us
    all_gather x1, blocking collectives, shards(): near = lax.all_gather(queries, 'zh', axis=0, tiled=True)  23.2 us
    gather x2, local copies, waits for them, and re-layouts, pair_products(): picked_docs = jnp.take(doc_side, pair_ids % local_blocks, axis=0)  18.8 us
  transfers between devices with their start and end apart: 3, of which 3 were waited for; matrix products, arithmetic and copies ran while one was open for 15% of the time, Pallas kernels for 0%

commit v1 on v0

--- a/solution.py
+++ b/solution.py
@@ -15,7 +15,9 @@
 
 
 def shards(queries, doc_vectors, surv_pairs, surv_count, short_pairs, short_count):
-    near = lax.all_gather(queries, "zh", axis=0, tiled=True)
+    near = jnp.concatenate(
+        lax.all_to_all(jnp.stack([queries] * lax.axis_size("zh")), "zh", 0, 0), axis=0
+    )
     every_query = lax.all_gather(near, ("y", "x"), axis=0, tiled=True)
     slice_width = queries.shape[1]
     query_blocks = every_query.reshape(-1, QB, slice_width)

time: 342 us -> 345 us (level)
  blocking collectives: 23.2 us -> 30.6 us
  waiting for transfers between devices: 226 us -> 222 us
    all_to_all x0 -> x1, blocking collectives: none -> 30.6 us  [shards(): lax.all_to_all(jnp.stack([queries] * lax.axis_size('zh')), 'zh', 0, 0)]
    all_gather x1 -> x0, blocking collectives: 23.2 us -> none  [shards(): near = lax.all_gather(queries, 'zh', axis=0, tiled=True)]
    all_gather x1, waiting for transfers between devices: 88.3 us -> 84.3 us  [shards(): every_query = lax.all_gather(near, ('y', 'x'), axis=0, tiled=True)]
where the time goes in v1:
time: 345 us
  waiting for transfers between devices  222 us (64%)
  local copies, waits for them, and re-layouts  44.6 us (13%)
  blocking collectives  30.6 us (9%)
  matrix products  25.2 us (7%)
  between operations  15.1 us (4%)
  other arithmetic  6.91 us (2%)
    reduce_scatter x1, waiting for transfers between devices, shards(): lax.psum_scatter(prefix_terms, DIMS, scatter_dimension=1, tiled=True)  104 us
    all_gather x1, waiting for transfers between devices, shards(): every_query = lax.all_gather(near, ('y', 'x'), axis=0, tiled=True)  84.3 us
    reduce_scatter x1, waiting for transfers between devices, shards(): lax.psum_scatter(full_terms, DIMS, scatter_dimension=1, tiled=True)  34 us
    all_to_all x1, blocking collectives, shards(): lax.all_to_all(jnp.stack([queries] * lax.axis_size('zh')), 'zh', 0, 0)  30.6 us
    gather x2, local copies, waits for them, and re-layouts, pair_products(): picked_queries = jnp.take(query_blocks, pair_ids // local_blocks, axis=0)  27.2 us
    dot_general x2, matrix products, pair_products(): jnp.einsum('gqc,gdc->gqd', picked_queries, picked_docs, preferred_element...  25.2 us
    gather x2, local copies, waits for them, and re-layouts, pair_products(): picked_docs = jnp.take(doc_side, pair_ids % local_blocks, axis=0)  17.4 us
  transfers between devices with their start and end apart: 3, of which 3 were waited for; matrix products, arithmetic and copies ran while one was open for 15% of the time, Pallas kernels for 0%

profile of v1, /device:TPU:2, one launch (start us, length us, event | category | flops | bytes accessed | tf_op | source)
XLA Modules:
  0.0 344.8 jit_solution(18074171448919336911)
XLA Ops:
  7.2 0.0 copy-start
  7.2 0.0 all-gather.2.cloned.1.call-start
  7.2 1.3 pad_maximum_fusion
  8.5 30.6 %all_to_all.5 = bf16[2,512,384]{2,1,0:T(8,128)(2,1)} all-to-all(bf16[2,512,384]{2,1,0:T(8,128)(2,1)S(1)} %pad_maximum_fusion), channel_id=1, replica_groups=mesh['y'=4,'x'=4,'zh'=2,'zl'=4,'c'=2] {'zh'}, dimensions={0} | all-to-all | bytes 1572864 | tf_op jit(solution)/shard_map/all_to_all | solution.py:19
  39.1 0.0 all-gather.2.cloned.1.call-update
  39.1 0.0 reduce-scatter.5.cloned.1.call-start
  39.2 0.7 fusion.12
  39.9 0.0 copy-done
  39.9 0.0 copy-start.2
  39.9 7.9 %gather_fusion.3 = bf16[96,128,384]{2,1,0:T(8,128)(2,1)} fusion(bf16[16,128,384]{2,1,0:T(8,128)(2,1)S(1)} %bitcast.67, s32[1024]{0:T(1024)S(1)} %get-tuple-element.10), kind=kCustom, calls=%fused_computation.3 | custom fusion | bytes 18874752 | tf_op jit(solution)/shard_map/jit(_take)/gather | solution.py:33
  47.8 84.3 %all-gather.2.cloned.1.call-done = bf16[16384,384]{1,0:T(8,128)(2,1)} async-done(((bf16[1024,384]{1,0:T(8,128)(2,1)}), bf16[16384,384]{1,0:T(8,128)(2,1)}) %all-gather.2.cloned.1.call-update) | async-done | bytes 12582928 | tf_op jit(solution)/shard_map/all_gather | solution.py:21
  132.1 12.5 %gather_fusion.2 = bf16[96,128,384]{2,1,0:T(8,128)(2,1)} fusion(bf16[128,128,384]{2,1,0:T(8,128)(2,1)} %bitcast.69, s32[1024]{0:T(1024)S(1)} %get-tuple-element.11), kind=kCustom, calls=%fused_computation.2 | custom fusion | bytes 18874752 | tf_op jit(solution)/shard_map/jit(_take)/gather | solution.py:32
  144.6 10.3 %fusion.5 = f32[96,128,128]{2,1,0:T(8,128)} fusion(bf16[96,128,384]{2,1,0:T(8,128)(2,1)} %gather_fusion.3, bf16[96,128,384]{2,1,0:T(8,128)(2,1)} %gather_fusion.2, pred[96]{0:T(512)(128)(4,1)S(1)} %get-tuple-element.7, pred[96]{0:T(512)(128)(4,1)S(1)} %get-tuple-element.6), kind=kOutput, calls=%fused_computation.9 | convolution fusion | flops 1217396736 | bytes 25166016 | tf_op jit(solution)/shard_map/gqc,gdc->gqd/dot_general | solution.py:34
  154.9 0.0 reduce-scatter.5.cloned.1.call-update
  155.0 0.2 reduce-scatter.3.cloned.1.call-start
  155.3 0.2 broadcast_select_fusion
  155.4 9.5 %gather_fusion.1 = bf16[144,128,384]{2,1,0:T(8,128)(2,1)} fusion(bf16[16,128,384]{2,1,0:T(8,128)(2,1)S(1)} %broadcast_select_fusion, s32[1024]{0:T(1024)S(1)} %pad_clamp_fusion.2), kind=kCustom, calls=%fused_computation.1 | custom fusion | bytes 28312128 | tf_op jit(solution)/shard_map/jit(_take)/gather | solution.py:33
  165.0 14.7 %gather_fusion = bf16[144,128,384]{2,1,0:T(8,128)(2,1)} fusion(bf16[128,128,384]{2,1,0:T(8,128)(2,1)} %bitcast.70, s32[1024]{0:T(1024)S(1)} %pad_clamp_fusion.3), kind=kCustom, calls=%fused_computation | custom fusion | bytes 28312128 | tf_op jit(solution)/shard_map/jit(_take)/gather | solution.py:32
  179.7 14.8 %fusion = f32[144,128,128]{2,1,0:T(8,128)} fusion(bf16[144,128,384]{2,1,0:T(8,128)(2,1)} %gather_fusion.1, bf16[144,128,384]{2,1,0:T(8,128)(2,1)} %gather_fusion, pred[144]{0:T(512)(128)(4,1)S(1)} %get-tuple-element.5, pred[144]{0:T(512)(128)(4,1)S(1)} %get-tuple-element.4), kind=kOutput, calls=%fused_computation.4 | convolution fusion | flops 1826095104 | bytes 37749024 | tf_op jit(solution)/shard_map/gqc,gdc->gqd/dot_general | solution.py:34
  194.5 0.0 reduce-scatter.3.cloned.1.call-update
  195.9 34.0 %reduce-scatter.5.cloned.1.call-done = f32[96,16,128]{2,1,0:T(8,128)} async-done(((f32[96,128,128]{2,1,0:T(8,128)}), f32[96,16,128]{2,1,0:T(8,128)}) %reduce-scatter.5.cloned.1.call-update) | async-done | bytes 786448 | tf_op jit(solution)/shard_map/reduce_scatter | solution.py:42
  229.9 2.2 select_bitcast_fusion.1
  232.1 103.7 %reduce-scatter.3.cloned.1.call-done = f32[144,16,128]{2,1,0:T(8,128)} async-done(((f32[144,128,128]{2,1,0:T(8,128)}), f32[144,16,128]{2,1,0:T(8,128)}) %reduce-scatter.3.cloned.1.call-update) | async-done | bytes 1179664 | tf_op jit(solution)/shard_map/reduce_scatter | solution.py:41
  335.8 2.5 select_bitcast_fusion
  (13 shorter events, 0.1 us)
Async XLA Ops:
  7.2 32.7 %copy-start = (bf16[2048,384]{1,0:T(8,128)(2,1)S(1)}, bf16[2048,384]{1,0:T(8,128)(2,1)}, u32[]{:S(2)}) copy-start(bf16[2048,384]{1,0:T(8,128)(2,1)} %param.7) | copy-start | bytes 4718596
  7.2 124.9 %all-gather.2.cloned.1.call-start = ((), (), s32[]{:S(2)}) async-start(), calls=%async_computation.3 | async-start | bytes 13369344 | tf_op jit(solution)/shard_map/all_gather | solution.py:21
  39.1 190.7 %reduce-scatter.5.cloned.1.call-start = ((), (), s32[]{:S(2)}) async-start(), calls=%async_computation.5 | async-start | bytes 7077888 | tf_op jit(solution)/shard_map/reduce_scatter | solution.py:42
  39.9 7.9 %copy-start.2 = (s32[1,96]{1,0:T(1,128)S(1)}, s32[1,96]{1,0:T(1,128)}, u32[]{:S(2)}) copy-start(s32[1,96]{1,0:T(1,128)} %param.10) | copy-start | bytes 1156
  144.6 10.6 %copy-start.1 = (s32[1,144]{1,0:T(1,128)S(1)}, s32[1,144]{1,0:T(1,128)}, u32[]{:S(2)}) copy-start(s32[1,144]{1,0:T(1,128)} %param.8) | copy-start | bytes 1732
  155.0 180.8 %reduce-scatter.3.cloned.1.call-start = ((), (), s32[]{:S(2)}) async-start(), calls=%async_computation.4 | async-start | bytes 10616832 | tf_op jit(solution)/shard_map/reduce_scatter | solution.py:41
Sparse Core Ops, SparseCore 0:
  39.3 92.7 all-gather.1
  155.1 74.7 reduce-scatter.4
  232.4 103.2 reduce-scatter.2
